TPU v7x, 32 devices: a whole 2x2x4 slice. The times are simulated.
32 devices in a mesh: groups: 2 (over y), sec: 4 (over x, core), plane: 4 (over z).
Axes of the slice: x: 2, y: 2, z: 4, core: 2. Of those that a mesh axis runs over, the one named last changes fastest.
Arguments:
- tokens: bfloat16 [16, 512, 1024], P(('groups', 'sec'), 'plane'), parts along dimension 0, may hold values from -8 to 8
- counts: int32 [16], P('groups'), parts along dimension 0, may hold values from 128 to 512, as said below
- region_ids: int32 [16, 512], P(('groups', 'sec'), 'plane'), parts along dimension 0, may hold values from 0 to 31
- norm_gains: float32 [2, 1024], replicated, may hold values from 0.1 to 1.9
- cross_qkv: bfloat16 [1024, 3072], P('plane'), may hold values from -2 to 2
- cross_out: bfloat16 [1024, 1024], P('plane'), may hold values from -0.1875 to 0.1875
- plane_qkv: bfloat16 [1024, 3072], P('plane'), may hold values from -2 to 2
- plane_out: bfloat16 [1024, 1024], P('plane'), may hold values from -0.1875 to 0.1875
Outputs:
- encoded: bfloat16 [16, 512, 1024], P(('groups', 'sec'), 'plane'), parts along dimension 0
- pooled: float32 [64, 1024], P(('groups', 'sec', 'plane')), parts along dimension 0
There are 2 independent parts, one for each index of `groups`. A program takes and returns all parts, laid end to end along the dimension named above; an argument that names none is the same for every part. Nothing has to cross between parts.
Inputs may be any that keep to these rules, and one draw needn't show every extreme that they name: `counts`: valid tissue tokens of each section; they are the first positions of the section.
All inputs are finite; a program needn't handle non-finite values.
Results may differ from a plain program's by a relative error of at most 0.009.
Values may be sent and summed in bfloat16 or wider, within the bound.
No kernel may reach another device: no remote copies, remote signals or barrier semaphores. Data moves between devices by JAX's collectives and lax.ppermute only.
A program may use at most 64 MiB of HBM per device.

v0:
```python
import math
import jax
import jax.numpy as jnp
from jax import lax
from jax.sharding import PartitionSpec as P

HEADS = 16
HEAD_DIM = 64
WINDOW = 128
negative_big = -1e30


def shifted_2(value, axis, by):
    peers = lax.axis_size(axis)
    pairs = [(i, i + by) for i in range(peers) if 0 <= i + by < peers]
    return lax.ppermute(value, axis, pairs)


def rms_norm(values, gain):
    wide = values.astype(jnp.float32)
    scaled = wide * lax.rsqrt(jnp.mean(wide * wide, axis=-1, keepdims=True) + 1e-06) * gain
    return scaled.astype(jnp.bfloat16)


def masked_softmax(scores, allowed):
    shifted = jnp.where(allowed, scores, negative_big)
    top = jnp.max(shifted, axis=-1, keepdims=True)
    expo = jnp.where(allowed, jnp.exp(shifted - top), 0.0)
    return (expo / jnp.sum(expo, axis=-1, keepdims=True)).astype(jnp.bfloat16)


def fold_product(inputs, weight_piece):
    return jnp.dot(inputs, weight_piece, preferred_element_type=jnp.float32)


def attend_items(pieces):
    packed_all, flags_all = pieces
    seq_len = packed_all.shape[2]
    block_len = 512
    score_scale = 1.0 / math.sqrt(HEAD_DIM)
    key_index = jnp.arange(seq_len, dtype=jnp.int32)

    def one_item(item_pair):
        packed, key_flag = item_pair
        key_rows = packed[:, HEAD_DIM : 2 * HEAD_DIM]
        value_rows = packed[:, 2 * HEAD_DIM :]
        key_alive = key_flag > 0.5
        query_blocks = packed[:, :HEAD_DIM].reshape(seq_len // block_len, block_len, HEAD_DIM)
        block_starts = jnp.arange(seq_len // block_len, dtype=jnp.int32) * block_len

        def one_block(block_pair):
            query_rows, offset = block_pair
            scores = (
                jnp.einsum("qd,kd->qk", query_rows, key_rows, preferred_element_type=jnp.float32)
                * score_scale
            )
            own_index = offset + jnp.arange(block_len, dtype=jnp.int32)
            allowed = key_alive[None, :] | (key_index[None, :] == own_index[:, None])
            attention = masked_softmax(scores, allowed)
            return jnp.dot(attention, value_rows, preferred_element_type=jnp.float32).astype(
                jnp.bfloat16
            )

        return lax.map(one_block, (query_blocks, block_starts)).reshape(seq_len, HEAD_DIM)

    return lax.map(one_item, (packed_all[0], flags_all[0]))[None]


def body(tokens, counts, region_ids, norm_gains, cross_qkv, cross_out, plane_qkv, plane_out):
    sec_block, tok_block, model_width = tokens.shape
    plane_count = lax.axis_size("plane")
    regions = 2 * lax.axis_size("sec") * plane_count
    positions = lax.axis_index("plane") * tok_block + jnp.arange(tok_block, dtype=jnp.int32)
    padded_counts = jnp.concatenate(
        [jnp.zeros((1,), jnp.int32), counts, jnp.zeros((1,), jnp.int32)]
    )
    near_counts = lax.dynamic_slice_in_dim(
        padded_counts, lax.axis_index("sec") * sec_block, sec_block + 2
    )
    near_valid = positions[None, :] < near_counts[:, None]
    own_valid = near_valid[1 : sec_block + 1]
    score_scale = 1.0 / math.sqrt(HEAD_DIM)
    normed = rms_norm(tokens, norm_gains[0])
    inputs = normed.reshape(-1, model_width)
    result = fold_product(inputs, lax.all_gather(cross_qkv, "plane", axis=0, tiled=True))
    projected = result.astype(jnp.bfloat16).reshape(sec_block, tok_block, 3 * model_width)
    own_kv = projected[:, :, model_width:]
    from_below = shifted_2(own_kv[sec_block - 1], "sec", 1)
    from_above = shifted_2(own_kv[0], "sec", -1)
    near_kv = jnp.concatenate([from_below[None], own_kv, from_above[None]], axis=0)
    queries = projected[:, :, :model_width]
    windows = tok_block // WINDOW
    query_win = queries.reshape(sec_block, windows, WINDOW, HEADS, HEAD_DIM)
    pair_win = near_kv.reshape(sec_block + 2, windows, WINDOW, 2, HEADS, HEAD_DIM)
    stacked = jnp.concatenate(
        [pair_win[0:sec_block], pair_win[1 : sec_block + 1], pair_win[2 : sec_block + 2]], axis=2
    )
    valid_win = near_valid.reshape(sec_block + 2, windows, WINDOW)
    valid_three = jnp.concatenate(
        [valid_win[0:sec_block], valid_win[1 : sec_block + 1], valid_win[2 : sec_block + 2]], axis=2
    )
    itself = jnp.arange(3 * WINDOW)[None, :] == jnp.arange(WINDOW)[:, None] + WINDOW
    scores = (
        jnp.einsum(
            "snqhd,snkhd->snhqk", query_win, stacked[:, :, :, 0], preferred_element_type=jnp.float32
        )
        * score_scale
    )
    allowed = valid_three[:, :, None, None, :] | itself[None, None, None]
    attention = masked_softmax(scores, allowed)
    context = jnp.einsum(
        "snhqk,snkhd->snqhd", attention, stacked[:, :, :, 1], preferred_element_type=jnp.float32
    )
    context = context.astype(jnp.bfloat16).reshape(-1, model_width)
    result = fold_product(context, lax.all_gather(cross_out, "plane", axis=0, tiled=True))
    after_cross = (tokens.reshape(-1, model_width).astype(jnp.float32) + result).astype(
        jnp.bfloat16
    )
    normed = rms_norm(after_cross, norm_gains[1])
    result = fold_product(normed, lax.all_gather(plane_qkv, "plane", axis=0, tiled=True))
    projected = result.astype(jnp.bfloat16).reshape(sec_block, tok_block, 3, HEADS, HEAD_DIM)
    per_device = sec_block * HEADS // plane_count
    heads_first = jnp.transpose(projected, (0, 3, 1, 2, 4)).reshape(
        plane_count, per_device, tok_block, 3 * HEAD_DIM
    )
    key_flags = jnp.broadcast_to(own_valid[:, None, :], (sec_block, HEADS, tok_block)).astype(
        jnp.bfloat16
    )
    key_flags = key_flags.reshape(plane_count, per_device, tok_block)
    attended = attend_items(
        (
            lax.all_to_all(heads_first, "plane", split_axis=0, concat_axis=2, tiled=True),
            lax.all_to_all(key_flags, "plane", split_axis=0, concat_axis=2, tiled=True),
        )
    )
    returned = lax.all_to_all(attended, "plane", split_axis=2, concat_axis=0, tiled=True)
    context = jnp.transpose(
        returned.reshape(sec_block, HEADS, tok_block, HEAD_DIM), (0, 2, 1, 3)
    ).reshape(-1, model_width)
    result = fold_product(context, lax.all_gather(plane_out, "plane", axis=0, tiled=True))
    encoded = (after_cross.astype(jnp.float32) + result).astype(jnp.bfloat16)
    labels = region_ids.reshape(-1)
    member = (jnp.arange(regions, dtype=jnp.int32)[:, None] == labels[None, :]) & own_valid.reshape(
        -1
    )[None, :]
    region_sum = jnp.dot(member.astype(jnp.bfloat16), encoded, preferred_element_type=jnp.float32)
    region_count = jnp.sum(member.astype(jnp.float32), axis=1)
    totals, counted = (
        lax.psum_scatter(region_sum, ("sec", "plane"), scatter_dimension=0, tiled=True),
        lax.psum_scatter(region_count, ("sec", "plane"), scatter_dimension=0, tiled=True),
    )
    pooled = totals / jnp.maximum(counted, 1.0)[:, None]
    return (encoded.reshape(sec_block, tok_block, model_width), pooled)


def solution(mesh):
    in_specs = (
        P(("groups", "sec"), "plane", None),
        P("groups"),
        P(("groups", "sec"), "plane"),
        P(),
        P("plane", None),
        P("plane", None),
        P("plane", None),
        P("plane", None),
    )
    out_specs = (P(("groups", "sec"), "plane", None), P(("groups", "sec", "plane"), None))
    return jax.shard_map(body, mesh=mesh, in_specs=in_specs, out_specs=out_specs, check_vma=False)
```

profile of v0, /device:TPU:8, one launch (start us, length us, event | category | flops | bytes accessed | tf_op | source)
XLA Modules:
  0.0 521.9 jit_solution(6824321501404920193)
XLA Ops:
  10.1 113.1 %all-gather.5.cloned.1.call-done = bf16[1024,3072]{1,0:T(8,128)(2,1)} async-done(((bf16[256,3072]{1,0:T(8,128)(2,1)}), bf16[1024,3072]{1,0:T(8,128)(2,1)}) %all-gather.5.cloned.1.call-update) | async-done | bytes 6291472 | tf_op jit(solution)/shard_map/all_gather | solution.py:85
  123.2 4.6 convolution_convert_fusion.2
  127.8 1.0 copy.72
  128.8 2.7 collective-permute-start
  131.5 1.0 copy.74
  132.6 1.3 collective-permute-start.1
  135.6 1.3 copy.58
  137.2 1.4 pad_maximum_fusion.2
  139.1 1.0 fusion.18
  140.1 3.2 fusion.43
  143.4 1.8 fusion.22
  145.8 24.5 %all-gather.7.cloned.1.call-done = bf16[1024,1024]{1,0:T(8,128)(2,1)} async-done(((bf16[256,1024]{1,0:T(8,128)(2,1)}), bf16[1024,1024]{1,0:T(8,128)(2,1)}) %all-gather.7.cloned.1.call-update) | async-done | bytes 2097168 | tf_op jit(solution)/shard_map/all_gather | solution.py:115
  170.3 2.4 fusion.23
  172.8 111.8 %all-gather.9.cloned.1.call-done = bf16[1024,3072]{1,0:T(8,128)(2,1)} async-done(((bf16[256,3072]{1,0:T(8,128)(2,1)}), bf16[1024,3072]{1,0:T(8,128)(2,1)}) %all-gather.9.cloned.1.call-update) | async-done | bytes 6291472 | tf_op jit(solution)/shard_map/all_gather | solution.py:120
  284.6 5.8 %convolution_convert_fusion.1 = bf16[256,3072]{1,0:T(8,128)(2,1)} fusion(bf16[1024,3072]{1,0:T(8,128)(2,1)} %all-gather.9.cloned.1.call-done, bf16[256,1024]{1,0:T(8,128)(2,1)S(1)} %get-tuple-element.97, f32[1024]{0:T(1024)S(1)} %bitcast.126, f32[256]{0:T(256)S(1)} %add_rsqrt_fusion), kind=kOutput, calls=%fused_computation.23 | convolution fusion | flops 1612447744 | bytes 8393728 | tf_op jit(solution)/shard_map/dot_general | solution.py:33
  290.4 1.7 copy.60
  293.0 41.6 %all_to_all.45 = bf16[4,8,128,192]{2,3,1,0:T(8,128)(2,1)S(1)} all-to-all(bf16[4,8,128,192]{2,3,1,0:T(8,128)(2,1)S(1)} %bitcast.105), channel_id=1, replica_groups=mesh['groups'=2,'sec'=4,'plane'=4] {'plane'}, dimensions={0} | all-to-all | bytes 3145728 | tf_op jit(solution)/shard_map/all_to_all | solution.py:132
  335.2 5.0 all-to-all-start
  340.8 2.5 copy.69
  343.3 1.1 all-to-all-done
  344.4 16.5 %while.11 = (s32[]{:T(128)}, bf16[8,512,64]{1,2,0:T(8,128)(2,1)S(1)}, bf16[8,512]{1,0:T(8,128)(2,1)S(1)}, bf16[8,512,192]{2,1,0:T(8,128)(2,1)}, s32[]{:T(128)}) while((s32[]{:T(128)}, bf16[8,512,64]{1,2,0:T(8,128)(2,1)S(1)}, bf16[8,512]{1,0:T(8,128)(2,1)S(1)}, bf16[8,512,192]{2,1,0:T(8,128)(2,1)}, s32[]{:T(128)}) %tuple.56), condition=%wide.region_7.8_spmd.clone, body=%wide.region_4.7_spmd.clone.sunk | while | flops 71336448 | bytes 3945545 | solution.py:66
  346.5 1.0 dynamic-slice_bitcast_fusion.2
  348.5 1.0 dynamic-slice_bitcast_fusion.2
  350.6 1.0 dynamic-slice_bitcast_fusion.2
  352.7 1.0 dynamic-slice_bitcast_fusion.2
  356.8 1.0 dynamic-slice_bitcast_fusion.2
  361.8 1.6 reshape.161
  363.3 5.0 all-to-all-start.2
  369.7 48.3 %all-reduce.1 = f32[32]{0:T(128)S(1)} all-reduce(f32[32]{0:T(128)S(1)} %convert_reduce_fusion), channel_id=3, replica_groups=mesh['groups'=2,'sec'=4,'plane'=4] {'sec','plane'}, use_global_device_ids=true, to_apply=%region_10.11.clone | all-reduce | flops 32 | bytes 256
  420.3 2.3 fusion.19
  423.6 90.4 %all-reduce.4.cloned.1.call-done = f32[32,1024]{1,0:T(8,128)} async-done(((f32[32,1024]{1,0:T(8,128)}), f32[32,1024]{1,0:T(8,128)}) %all-reduce.4.cloned.1.call-update) | async-done | bytes 131088
  514.0 1.4 dynamic-slice_divide_fusion
  (100 shorter events, 24.0 us)
Async XLA Ops:
  7.2 2.3 copy-start.6
  7.2 2.5 copy-start
  7.2 2.7 copy-start.4
  7.2 116.0 %all-gather.5.cloned.1.call-start = ((), (), s32[]{:S(2)}) async-start(), calls=%async_computation.3 | async-start | bytes 7864320 | tf_op jit(solution)/shard_map/all_gather | solution.py:85
  7.9 162.4 %all-gather.7.cloned.1.call-start = ((), (), s32[]{:S(2)}) async-start(), calls=%async_computation.4 | async-start | bytes 2621440 | tf_op jit(solution)/shard_map/all_gather | solution.py:115
  8.7 275.9 %all-gather.9.cloned.1.call-start = ((), (), s32[]{:S(2)}) async-start(), calls=%async_computation.5 | async-start | bytes 7864320 | tf_op jit(solution)/shard_map/all_gather | solution.py:120
  128.8 8.1 %collective-permute-start = (bf16[128,2048]{0,1:T(8,128)(2,1)}, bf16[128,2048]{0,1:T(8,128)(2,1)}, u32[]{:S(2)}, u32[]{:S(2)}) collective-permute-start(bf16[128,2048]{0,1:T(8,128)(2,1)} %bitcast.121), channel_id=1, source_target_pairs={{0,4},{4,8},{8,12},{1,5},{5,9},{9,13},{2,6},{6,10},{10,14},{3,7},{... | collective-permute-start | bytes 1572872 | tf_op jit(solution)/shard_map/ppermute | solution.py:16
  132.6 4.7 collective-permute-start.1
  172.7 117.7 %copy-start.2 = (bf16[256,1024]{1,0:T(8,128)(2,1)}, bf16[256,1024]{1,0:T(8,128)(2,1)S(1)}, u32[]{:S(2)}) copy-start(bf16[256,1024]{1,0:T(8,128)(2,1)S(1)} %get-tuple-element.97) | copy-start | bytes 1572868
  335.2 9.2 %all-to-all-start = ((bf16[4,8,128]{2,1,0:T(8,128)(2,1)}), bf16[4,8,128]{2,1,0:T(8,128)(2,1)S(1)}, u32[]{:S(2)}, u32[]{:S(2)}) async-start(bf16[4,8,128]{2,1,0:T(8,128)(2,1)} %broadcast_in_dim.86), calls=%async_computation | async-start | bytes 16384 | tf_op jit(solution)/shard_map/all_to_all | solution.py:133
  340.2 80.1 %all-gather.11.cloned.1.call-start = ((), (), s32[]{:S(2)}) async-start(), calls=%async_computation.6 | async-start | bytes 2621440 | tf_op jit(solution)/shard_map/all_gather | solution.py:140
  360.9 7.4 %copy-start.7 = (u32[32]{0:T(128)S(1)}, u32[32]{0:T(128)}, u32[]{:S(2)}) copy-start(u32[32]{0:T(128)} %constant.80) | copy-start | bytes 388
  360.9 8.7 %copy-start.5 = (s32[2,128]{1,0:T(2,128)S(1)}, s32[2,128]{1,0:T(2,128)}, u32[]{:S(2)}) copy-start(s32[2,128]{1,0:T(2,128)} %param.12) | copy-start | bytes 3076
  363.3 56.9 %copy-start.3 = (bf16[256,1024]{1,0:T(8,128)(2,1)S(1)}, bf16[256,1024]{1,0:T(8,128)(2,1)}, u32[]{:S(2)}) copy-start(bf16[256,1024]{1,0:T(8,128)(2,1)} %copy-done.2) | copy-start | bytes 1572868
  363.3 54.7 %all-to-all-start.2 = ((bf16[4,2,32768]{2,1,0:T(2,128)(2,1)}), bf16[4,2,32768]{2,1,0:T(2,128)(2,1)S(1)}, u32[]{:S(2)}, u32[]{:S(2)}) async-start(bf16[4,2,32768]{2,1,0:T(2,128)(2,1)} %reshape.161), calls=%async_computation.2 | async-start | bytes 1048576 | tf_op jit(solution)/shard_map/all_to_all | solution.py:136
  368.3 145.6 %all-reduce.4.cloned.1.call-start = ((), (), s32[]{:S(2)}) async-start(), calls=%async_computation.7 | async-start | bytes 262144
  422.6 92.8 %copy-start.1 = (bf16[256,1024]{1,0:T(8,128)(2,1)}, bf16[256,1024]{1,0:T(8,128)(2,1)S(1)}, u32[]{:S(2)}) copy-start(bf16[256,1024]{1,0:T(8,128)(2,1)S(1)} %fusion.19) | copy-start | bytes 1572868
Sparse Core Ops, SparseCore 0:
  9.6 113.5 all-gather.4
  124.7 45.5 all-gather.6
  171.9 112.6 all-gather.8
  342.3 54.9 all-gather.10
  423.6 90.2 all-reduce.3
where the time goes:
time: 523 us; the launch traced here: 522 us
  waiting for transfers between devices  344 us (66%)
  blocking collectives  89.9 us (17%)
  matrix products  25.1 us (5%)
  local copies, waits for them, and re-layouts  24.3 us (5%)
  between operations  14.8 us (3%)
  starting transfers between devices  14.1 us (3%)
  other arithmetic  9.64 us (2%)
    all_gather x1, waiting for transfers between devices, body(): lax.all_gather(cross_qkv, 'plane', axis=0, tiled=True)  113 us
    all_gather x1, waiting for transfers between devices, body(): lax.all_gather(plane_qkv, 'plane', axis=0, tiled=True)  112 us
    unnamed x6, waiting for transfers between devices  93 us
    unnamed x1, blocking collectives  48.3 us
    all_to_all x1, blocking collectives, body(): lax.all_to_all(heads_first, 'plane', split_axis=0, concat_axis=2, tiled=T...  41.6 us
    all_gather x1, waiting for transfers between devices, body(): lax.all_gather(cross_out, 'plane', axis=0, tiled=True)  24.5 us
    dot_general x4, matrix products, fold_product(): return jnp.dot(inputs, weight_piece, preferred_element_type=jnp.float32)  15.1 us
  transfers between devices with their start and end apart: 9, of which 6 were waited for; matrix products, arithmetic and copies ran while one was open for 9% of the time, Pallas kernels for 0%

commit v1 on v0

--- a/solution.py
+++ b/solution.py
@@ -1,3 +1,4 @@
+import functools
 import math
 import jax
 import jax.numpy as jnp
@@ -8,6 +9,36 @@
 HEAD_DIM = 64
 WINDOW = 128
 negative_big = -1e30
+
+
+def note_the_plate(x_part, mesh_dim):
+    near = lax.axis_size(mesh_dim)
+    prior = lax.axis_index(mesh_dim)
+    block_out, base_arr, arr_next = (near, prior, x_part.shape[0])
+    found = [num * block_out if j0 == 0 else num for j0, num in enumerate(x_part.shape)]
+    arr_now = jnp.zeros(found, x_part.dtype)
+    lower = lax.dynamic_update_slice_in_dim(arr_now, x_part, base_arr * arr_next, axis=0)
+    state_now = frame_out = x_part
+    for w in range(1, block_out // 2 + 1):
+        fresh = range(block_out)
+        d_next = map(lambda j0: (j0, (j0 + 1) % block_out), fresh)
+        k_now = list(d_next)
+        state_now = lax.ppermute(state_now, mesh_dim, k_now)
+        lower = lax.dynamic_update_slice_in_dim(
+            lower, state_now, (base_arr - w) % block_out * arr_next, axis=0
+        )
+        if 2 * w < block_out:
+            x_next = range(block_out)
+            main = map(lambda j0: (j0, (j0 - 1) % block_out), x_next)
+            last = list(main)
+            frame_out = lax.ppermute(frame_out, mesh_dim, last)
+            lower = lax.dynamic_update_slice_in_dim(
+                lower, frame_out, (base_arr + w) % block_out * arr_next, axis=0
+            )
+    return lower
+
+
+turn_lanes = functools.partial(note_the_plate, mesh_dim="plane")
 
 
 def shifted_2(value, axis, by):
@@ -82,7 +113,7 @@
     score_scale = 1.0 / math.sqrt(HEAD_DIM)
     normed = rms_norm(tokens, norm_gains[0])
     inputs = normed.reshape(-1, model_width)
-    result = fold_product(inputs, lax.all_gather(cross_qkv, "plane", axis=0, tiled=True))
+    result = fold_product(inputs, turn_lanes(cross_qkv))
     projected = result.astype(jnp.bfloat16).reshape(sec_block, tok_block, 3 * model_width)
     own_kv = projected[:, :, model_width:]
     from_below = shifted_2(own_kv[sec_block - 1], "sec", 1)

time: 523 us -> 484 us (0.925)
  waiting for transfers between devices: 344 us -> 282 us
  starting transfers between devices: 14.1 us -> 36.4 us
    ppermute x0 -> x3, waiting for transfers between devices: none -> 180 us  [the longest x2 173 us: note_the_plate(): state_now = lax.ppermute(state_now, mesh_dim, k_now)]
    all_gather x1 -> x0, waiting for transfers between devices: 113 us -> none  [body(): lax.all_gather(cross_qkv, 'plane', axis=0, tiled=True)]
    all_gather x1, waiting for transfers between devices: 112 us -> 8.1 us  [body(): lax.all_gather(plane_qkv, 'plane', axis=0, tiled=True)]
    all_gather x1, waiting for transfers between devices: 24.5 us -> 0.02 us  [body(): lax.all_gather(cross_out, 'plane', axis=0, tiled=True)]
    ppermute x0 -> x3, starting transfers between devices: none -> 22.8 us  [the longest x2 22.4 us: note_the_plate(): state_now = lax.ppermute(state_now, mesh_dim, k_now)]
    unnamed x6 -> x5, waiting for transfers between devices: 93 us -> 91.5 us
  transfers between devices with their start and end apart: 9 -> 11, of which waited for: 6 -> 7; matrix products, arithmetic and copies ran while one was open for 9% -> 10% of each run, Pallas kernels for 0% -> 0%
where the time goes in v1:
time: 484 us; the launch traced here: 483 us
  waiting for transfers between devices  282 us (58%)
  blocking collectives  88.8 us (18%)
  starting transfers between devices  36.4 us (8%)
  local copies, waits for them, and re-layouts  26.1 us (5%)
  matrix products  22.4 us (5%)
  between operations  14.9 us (3%)
  other arithmetic  12.4 us (3%)
    ppermute x2, waiting for transfers between devices, note_the_plate(): state_now = lax.ppermute(state_now, mesh_dim, k_now)  173 us
    unnamed x5, waiting for transfers between devices  91.5 us
    unnamed x1, blocking collectives  48.5 us
    all_to_all x1, blocking collectives, body(): lax.all_to_all(heads_first, 'plane', split_axis=0, concat_axis=2, tiled=T...  40.3 us
    ppermute x2, starting transfers between devices, note_the_plate(): state_now = lax.ppermute(state_now, mesh_dim, k_now)  22.4 us
    dot_general x4, matrix products, fold_product(): return jnp.dot(inputs, weight_piece, preferred_element_type=jnp.float32)  12.4 us
  transfers between devices with their start and end apart: 11, of which 7 were waited for; matrix products, arithmetic and copies ran while one was open for 10% of the time, Pallas kernels for 0%

profile of v1, /device:TPU:8, one launch (start us, length us, event | category | flops | bytes accessed | tf_op | source)
XLA Modules:
  0.0 483.1 jit_solution(2244698668681559025)
XLA Ops:
  8.7 1.6 collective-permute-start
  11.6 1.2 multiply_reduce_fusion
  13.7 81.8 %collective-permute-done = bf16[256,3072]{1,0:T(8,128)(2,1)S(1)} collective-permute-done((bf16[256,3072]{1,0:T(8,128)(2,1)}, bf16[256,3072]{1,0:T(8,128)(2,1)S(1)}, u32[]{:S(2)}, u32[]{:S(2)}) %collective-permute-start) | collective-permute-done | bytes 1572896 | tf_op jit(solution)/shard_map/ppermute | solution.py:26
  95.6 20.7 %collective-permute-start.2 = (bf16[256,3072]{1,0:T(8,128)(2,1)S(1)}, bf16[256,3072]{1,0:T(8,128)(2,1)S(1)}, u32[]{:S(2)}, u32[]{:S(2)}) collective-permute-start(bf16[256,3072]{1,0:T(8,128)(2,1)S(1)} %collective-permute-done), channel_id=1, source_target_pairs={{0,1},{1,2},{2,3},{3,0},{4,5},{5,6},{6,7},{7,4},{8,9},{9,10},{10,1... | collective-permute-start | bytes 4718600 | tf_op jit(solution)/shard_map/ppermute | solution.py:26
  116.3 1.2 multiply_convert_fusion
  118.7 6.2 %collective-permute-done.1 = bf16[256,3072]{1,0:T(8,128)(2,1)} collective-permute-done((bf16[256,3072]{1,0:T(8,128)(2,1)}, bf16[256,3072]{1,0:T(8,128)(2,1)}, u32[]{:S(2)}, u32[]{:S(2)}) %collective-permute-start.1) | collective-permute-done | bytes 1572896 | tf_op jit(solution)/shard_map/ppermute | solution.py:34
  124.9 1.6 constant_dynamic-update-slice_fusion.1
  126.5 91.5 %collective-permute-done.2 = bf16[256,3072]{1,0:T(8,128)(2,1)S(1)} collective-permute-done((bf16[256,3072]{1,0:T(8,128)(2,1)S(1)}, bf16[256,3072]{1,0:T(8,128)(2,1)S(1)}, u32[]{:S(2)}, u32[]{:S(2)}) %collective-permute-start.2) | collective-permute-done | bytes 1572896 | tf_op jit(solution)/shard_map/ppermute | solution.py:26
  218.2 1.8 convolution_convert_fusion.2
  220.2 1.0 copy.72
  221.2 2.1 collective-permute-start.3
  223.3 1.0 copy.74
  224.3 1.5 collective-permute-start.4
  227.0 1.8 collective-permute-done.4
  228.8 1.4 pad_maximum_fusion.2
  230.7 1.0 fusion.18
  231.7 3.2 fusion.43
  235.0 1.8 fusion.22
  237.4 2.4 fusion.23
  239.9 8.1 %all-gather.6.cloned.1.call-done = bf16[1024,3072]{1,0:T(8,128)(2,1)} async-done(((bf16[256,3072]{1,0:T(8,128)(2,1)}), bf16[1024,3072]{1,0:T(8,128)(2,1)}) %all-gather.6.cloned.1.call-update) | async-done | bytes 6291472 | tf_op jit(solution)/shard_map/all_gather | solution.py:151
  248.0 5.8 %convolution_convert_fusion.1 = bf16[256,3072]{1,0:T(8,128)(2,1)} fusion(bf16[1024,3072]{1,0:T(8,128)(2,1)} %all-gather.6.cloned.1.call-done, bf16[256,1024]{1,0:T(8,128)(2,1)S(1)} %get-tuple-element.97, f32[1024]{0:T(1024)S(1)} %bitcast.125, f32[256]{0:T(256)S(1)} %add_rsqrt_fusion), kind=kOutput, calls=%fused_computation.23 | convolution fusion | flops 1612447744 | bytes 8393728 | tf_op jit(solution)/shard_map/dot_general | solution.py:64
  253.8 1.7 copy.60
  256.3 40.3 %all_to_all.45 = bf16[4,8,128,192]{2,3,1,0:T(8,128)(2,1)S(1)} all-to-all(bf16[4,8,128,192]{2,3,1,0:T(8,128)(2,1)S(1)} %bitcast.105), channel_id=1, replica_groups=mesh['groups'=2,'sec'=4,'plane'=4] {'plane'}, dimensions={0} | all-to-all | bytes 3145728 | tf_op jit(solution)/shard_map/all_to_all | solution.py:163
  297.3 5.0 %all-to-all-start = ((bf16[4,8,128]{2,1,0:T(8,128)(2,1)}), bf16[4,8,128]{2,1,0:T(8,128)(2,1)S(1)}, u32[]{:S(2)}, u32[]{:S(2)}) async-start(bf16[4,8,128]{2,1,0:T(8,128)(2,1)} %broadcast_in_dim.90), calls=%async_computation | async-start | bytes 16384 | tf_op jit(solution)/shard_map/all_to_all | solution.py:164
  303.0 2.6 copy.69
  306.5 16.5 %while.11 = (s32[]{:T(128)}, bf16[8,512,64]{1,2,0:T(8,128)(2,1)S(1)}, bf16[8,512]{1,0:T(8,128)(2,1)S(1)}, bf16[8,512,192]{2,1,0:T(8,128)(2,1)}, s32[]{:T(128)}) while((s32[]{:T(128)}, bf16[8,512,64]{1,2,0:T(8,128)(2,1)S(1)}, bf16[8,512]{1,0:T(8,128)(2,1)S(1)}, bf16[8,512,192]{2,1,0:T(8,128)(2,1)}, s32[]{:T(128)}) %tuple.54), condition=%wide.region_7.8_spmd.clone, body=%wide.region_4.7_spmd.clone.sunk | while | flops 71336448 | bytes 3945545 | solution.py:97
  323.9 1.6 reshape.161
  325.4 4.9 %all-to-all-start.2 = ((bf16[4,2,32768]{2,1,0:T(2,128)(2,1)}), bf16[4,2,32768]{2,1,0:T(2,128)(2,1)S(1)}, u32[]{:S(2)}, u32[]{:S(2)}) async-start(bf16[4,2,32768]{2,1,0:T(2,128)(2,1)} %reshape.161), calls=%async_computation.2 | async-start | bytes 1048576 | tf_op jit(solution)/shard_map/all_to_all | solution.py:167
  331.7 48.5 %all-reduce.1 = f32[32]{0:T(128)S(1)} all-reduce(f32[32]{0:T(128)S(1)} %convert_reduce_fusion), channel_id=3, replica_groups=mesh['groups'=2,'sec'=4,'plane'=4] {'sec','plane'}, use_global_device_ids=true, to_apply=%region_10.11.clone | all-reduce | flops 32 | bytes 256
  382.5 2.3 fusion.19
  385.8 89.4 %all-reduce.4.cloned.1.call-done = f32[32,1024]{1,0:T(8,128)} async-done(((f32[32,1024]{1,0:T(8,128)}), f32[32,1024]{1,0:T(8,128)}) %all-reduce.4.cloned.1.call-update) | async-done | bytes 131088
  475.2 1.4 dynamic-slice_divide_fusion
  (106 shorter events, 31.3 us)
Async XLA Ops:
  7.2 111.1 %copy-start.4 = (bf16[256,3072]{1,0:T(8,128)(2,1)S(1)}, bf16[256,3072]{1,0:T(8,128)(2,1)}, u32[]{:S(2)}) copy-start(bf16[256,3072]{1,0:T(8,128)(2,1)} %param.14) | copy-start | bytes 4718596
  7.2 230.2 %all-gather.4.cloned.1.call-start = ((), (), s32[]{:S(2)}) async-start(), calls=%async_computation.3 | async-start | bytes 2621440 | tf_op jit(solution)/shard_map/all_gather | solution.py:146
  7.9 240.1 %all-gather.6.cloned.1.call-start = ((), (), s32[]{:S(2)}) async-start(), calls=%async_computation.4 | async-start | bytes 7864320 | tf_op jit(solution)/shard_map/all_gather | solution.py:151
  8.7 86.9 %collective-permute-start = (bf16[256,3072]{1,0:T(8,128)(2,1)}, bf16[256,3072]{1,0:T(8,128)(2,1)S(1)}, u32[]{:S(2)}, u32[]{:S(2)}) collective-permute-start(bf16[256,3072]{1,0:T(8,128)(2,1)} %param.14), channel_id=1, source_target_pairs={{0,1},{1,2},{2,3},{3,0},{4,5},{5,6},{6,7},{7,4},{8,9},{9,10},{10,1... | collective-permute-start | bytes 4718600 | tf_op jit(solution)/shard_map/ppermute | solution.py:26
  10.3 114.6 %collective-permute-start.1 = (bf16[256,3072]{1,0:T(8,128)(2,1)}, bf16[256,3072]{1,0:T(8,128)(2,1)}, u32[]{:S(2)}, u32[]{:S(2)}) collective-permute-start(bf16[256,3072]{1,0:T(8,128)(2,1)} %param.14), channel_id=1, source_target_pairs={{0,3},{1,0},{2,1},{3,2},{4,7},{5,4},{6,5},{7,6},{8,11},{9,8},{10,9... | collective-permute-start | bytes 4718600 | tf_op jit(solution)/shard_map/ppermute | solution.py:34
  95.6 122.5 %collective-permute-start.2 = (bf16[256,3072]{1,0:T(8,128)(2,1)S(1)}, bf16[256,3072]{1,0:T(8,128)(2,1)S(1)}, u32[]{:S(2)}, u32[]{:S(2)}) collective-permute-start(bf16[256,3072]{1,0:T(8,128)(2,1)S(1)} %collective-permute-done), channel_id=1, source_target_pairs={{0,1},{1,2},{2,3},{3,0},{4,5},{5,6},{6,7},{7,4},{8,9},{9,10},{10,1... | collective-permute-start | bytes 4718600 | tf_op jit(solution)/shard_map/ppermute | solution.py:26
  221.2 5.8 %collective-permute-start.3 = (bf16[128,2048]{0,1:T(8,128)(2,1)}, bf16[128,2048]{0,1:T(8,128)(2,1)}, u32[]{:S(2)}, u32[]{:S(2)}) collective-permute-start(bf16[128,2048]{0,1:T(8,128)(2,1)} %bitcast.4), channel_id=1, source_target_pairs={{0,4},{4,8},{8,12},{1,5},{5,9},{9,13},{2,6},{6,10},{10,14},{3,7},{... | collective-permute-start | bytes 1572872 | tf_op jit(solution)/shard_map/ppermute | solution.py:47
  224.3 4.6 collective-permute-start.4
  235.0 2.4 copy-start
  239.9 13.9 %copy-start.2 = (bf16[256,1024]{1,0:T(8,128)(2,1)}, bf16[256,1024]{1,0:T(8,128)(2,1)S(1)}, u32[]{:S(2)}) copy-start(bf16[256,1024]{1,0:T(8,128)(2,1)S(1)} %get-tuple-element.97) | copy-start | bytes 1572868
  297.3 9.2 %all-to-all-start = ((bf16[4,8,128]{2,1,0:T(8,128)(2,1)}), bf16[4,8,128]{2,1,0:T(8,128)(2,1)S(1)}, u32[]{:S(2)}, u32[]{:S(2)}) async-start(bf16[4,8,128]{2,1,0:T(8,128)(2,1)} %broadcast_in_dim.90), calls=%async_computation | async-start | bytes 16384 | tf_op jit(solution)/shard_map/all_to_all | solution.py:164
  302.3 80.2 %all-gather.8.cloned.1.call-start = ((), (), s32[]{:S(2)}) async-start(), calls=%async_computation.5 | async-start | bytes 2621440 | tf_op jit(solution)/shard_map/all_gather | solution.py:171
  322.9 7.3 %copy-start.6 = (u32[32]{0:T(128)S(1)}, u32[32]{0:T(128)}, u32[]{:S(2)}) copy-start(u32[32]{0:T(128)} %constant.111) | copy-start | bytes 388
  323.0 8.6 %copy-start.5 = (s32[2,128]{1,0:T(2,128)S(1)}, s32[2,128]{1,0:T(2,128)}, u32[]{:S(2)}) copy-start(s32[2,128]{1,0:T(2,128)} %param.12) | copy-start | bytes 3076
  323.0 59.5 %copy-start.3 = (bf16[256,1024]{1,0:T(8,128)(2,1)S(1)}, bf16[256,1024]{1,0:T(8,128)(2,1)}, u32[]{:S(2)}) copy-start(bf16[256,1024]{1,0:T(8,128)(2,1)} %copy-done.2) | copy-start | bytes 1572868
  325.4 54.8 %all-to-all-start.2 = ((bf16[4,2,32768]{2,1,0:T(2,128)(2,1)}), bf16[4,2,32768]{2,1,0:T(2,128)(2,1)S(1)}, u32[]{:S(2)}, u32[]{:S(2)}) async-start(bf16[4,2,32768]{2,1,0:T(2,128)(2,1)} %reshape.161), calls=%async_computation.2 | async-start | bytes 1048576 | tf_op jit(solution)/shard_map/all_to_all | solution.py:167
  330.3 144.9 %all-reduce.4.cloned.1.call-start = ((), (), s32[]{:S(2)}) async-start(), calls=%async_computation.6 | async-start | bytes 262144
  384.8 91.8 %copy-start.1 = (bf16[256,1024]{1,0:T(8,128)(2,1)}, bf16[256,1024]{1,0:T(8,128)(2,1)S(1)}, u32[]{:S(2)}) copy-start(bf16[256,1024]{1,0:T(8,128)(2,1)S(1)} %fusion.19) | copy-start | bytes 1572868
Sparse Core Ops, SparseCore 0:
  9.6 87.1 all-gather.3
  98.3 149.5 all-gather.5
  304.7 54.9 all-gather.7
  385.8 89.3 all-reduce.3
